TPU v7x, 256 devices: a whole 4x4x8 slice. The times are simulated.
256 devices in a mesh: tile: 16 (over z, core), tensor: 16 (over y, x).
Axes of the slice: x: 4, y: 4, z: 8, core: 2. Of those that a mesh axis runs over, the one named last changes fastest.
Arguments:
- image_hidden: bfloat16 [8, 32, 32, 3072], P(None, 'tile', 'tensor'), may hold values from -6 to 6
- text_hidden: bfloat16 [8, 512, 3072], P(None, ('tile', 'tensor')), may hold values from -6 to 6
- latents: float32 [8, 32, 2048], P(None, 'tile', 'tensor'), may hold values from -6 to 6
- step_index: int32 [8], replicated, may hold values from 0 to 27
- anchor: int32 [8, 2], replicated, may hold values from 0 to 63
- text_len: int32 [8], replicated, may hold values from 64 to 512
- mod_image: float32 [8, 3, 3072], replicated, may hold values from -3 to 3
- mod_text: float32 [8, 3, 3072], replicated, may hold values from -3 to 3
- mod_mlp: float32 [8, 3, 3072], replicated, may hold values from -3 to 3
- mod_final: float32 [8, 2, 3072], replicated, may hold values from -3 to 3
- qkv_image: bfloat16 [3072, 3, 2048], P(None, None, 'tensor'), may hold values from -0.109375 to 0.109375
- qkv_text: bfloat16 [3072, 3, 2048], P(None, None, 'tensor'), may hold values from -0.109375 to 0.109375
- proj_image: bfloat16 [2048, 3072], P('tensor'), may hold values from -0.125 to 0.125
- proj_text: bfloat16 [2048, 3072], P('tensor'), may hold values from -0.125 to 0.125
- qk_gain: float32 [2, 2, 128], replicated, may hold values from 0.5 to 10
- mlp_expand: bfloat16 [3072, 6144], P(None, 'tensor'), may hold values from -0.109375 to 0.109375
- mlp_reduce: bfloat16 [6144, 3072], P('tensor'), may hold values from -0.078125 to 0.078125
- final_weight: bfloat16 [3072, 64], replicated, may hold values from -0.109375 to 0.109375
Outputs:
- image_out: bfloat16 [8, 32, 32, 3072], P(None, 'tile', 'tensor')
- text_out: bfloat16 [8, 512, 3072], P(None, ('tile', 'tensor'))
- latents_ext: float32 [8, 64, 2048], P(None, 'tile', 'tensor')
Inputs may be any that keep to these rules, and one draw needn't show every extreme that they name: text_len gives each request's live text tokens; slots at or past it take no part as keys. step_index is a step of the 28-step plan.
All inputs are finite; a program needn't handle non-finite values.
Results may differ from a plain program's by a relative error of at most 0.0085.
The roundings to bfloat16 on the way count: a program that leaves them out, or rounds other values in their place, can miss the bound.
Values may be sent and summed in bfloat16 or wider, within the bound.
No kernel may reach another device: no remote copies, remote signals or barrier semaphores. Data moves between devices by JAX's collectives and lax.ppermute only.
A program may use at most 128 MiB of HBM per device.

v0:
```python
import math
import jax
import jax.numpy as jnp
from jax import lax
from jax.sharding import PartitionSpec as P

HEAD_DIM = 128
GRID = 32
NSTEPS = 28
norm_eps = 1e-06
time_shift = 3.0


def padded(value, sides, width):
    for axis, dim in sides:
        size, length = (lax.axis_size(axis), value.shape[dim])
        up = [(i, (i + 1) % size) for i in range(size - 1)]
        down = [(j, i) for i, j in up]
        last = lax.slice_in_dim(value, length - width, length, axis=dim)
        leading = lax.slice_in_dim(value, 0, width, axis=dim)
        before = lax.ppermute(last, axis, up)
        after = lax.ppermute(leading, axis, down)
        value = jnp.concatenate([before, value, after], axis=dim)
    return value


def layer_norm(values):
    average = jnp.mean(values, -1, keepdims=True)
    centred = values - average
    spread = jnp.mean(centred * centred, -1, keepdims=True)
    return centred * lax.rsqrt(spread + norm_eps)


def modulate(hidden, shift, stretch):
    normed = layer_norm(hidden.astype(jnp.float32))
    return ((1.0 + stretch) * normed + shift).astype(jnp.bfloat16)


def rope_tables(row_ids, col_ids):
    lane = jnp.arange(2 * 64, dtype=jnp.int32)
    pair_index = lane // 2
    row_rank = (pair_index - 8).astype(jnp.float32)
    col_rank = (pair_index - 36).astype(jnp.float32)
    log_base = math.log(10000.0)
    row_freq = jnp.where(
        (pair_index >= 8) & (pair_index < 36), jnp.exp(-2.0 * row_rank / 56.0 * log_base), 0.0
    )
    col_freq = jnp.where(pair_index >= 36, jnp.exp(-2.0 * col_rank / 56.0 * log_base), 0.0)
    angles = row_ids[..., None] * row_freq + col_ids[..., None] * col_freq
    sign_table = jnp.where(lane % 2 == 0, -1.0, 1.0).astype(jnp.float32)
    return (jnp.cos(angles), jnp.sin(angles) * sign_table)


def rotate(values, cos_table, sin_table):
    lane = lax.broadcasted_iota(jnp.int32, values.shape, values.ndim - 1)
    swapped = jnp.where(lane % 2 == 0, jnp.roll(values, -1, axis=-1), jnp.roll(values, 1, axis=-1))
    return values * cos_table + swapped * sin_table


def head_norm(projected, head_gain):
    squares = jnp.mean(projected * projected, -1, keepdims=True)
    return projected * lax.rsqrt(squares + norm_eps) * head_gain


def sigma_of(step_float):
    level = 1.0 - step_float / NSTEPS
    return time_shift * level / (1.0 + (time_shift - 1.0) * level)


def key_usable(text_len, key_count, text_tile, block_len):
    key_pos = jnp.arange(key_count, dtype=jnp.int32)
    owner_tile = key_pos // block_len
    offset = key_pos % block_len
    text_pos = owner_tile * text_tile + offset
    return jnp.logical_or(offset[None, :] >= text_tile, text_pos[None, :] < text_len[:, None])


def sum_over_tensor(term, owners, narrow):
    if not narrow:
        return lax.psum_scatter(term, "tensor", scatter_dimension=0, tiled=True)
    parts = term.astype(jnp.bfloat16).reshape((owners, -1) + term.shape[1:])
    parts = lax.all_to_all(parts, "tensor", 0, 0, tiled=True)
    return jnp.sum(parts.astype(jnp.float32), 0)


NARROW_SUMS = True


def per_device(
    image_hidden,
    text_hidden,
    latents,
    step_index,
    anchor,
    text_len,
    mod_image,
    mod_text,
    mod_mlp,
    mod_final,
    qkv_image,
    qkv_text,
    proj_image,
    proj_text,
    qk_gain,
    mlp_expand,
    mlp_reduce,
    final_weight,
):
    requests, tile_rows, tile_cols, model_width = image_hidden.shape
    local_cols = qkv_image.shape[2]
    local_heads = local_cols // HEAD_DIM
    owners = lax.axis_size("tensor")
    own_image = tile_rows * tile_cols
    own_text = text_hidden.shape[1]
    slots = own_image + own_text
    image_own = image_hidden.reshape(requests, own_image, model_width).transpose(1, 0, 2)
    text_own = text_hidden.transpose(1, 0, 2)
    image_mod_own = modulate(image_own, mod_image[None, :, 0, :], mod_image[None, :, 1, :])
    text_mod_own = modulate(text_own, mod_text[None, :, 0, :], mod_text[None, :, 1, :])
    image_count = owners * own_image
    text_tile = owners * own_text
    block_len = text_tile + image_count
    image_mod = lax.all_gather(image_mod_own, "tensor", axis=0, tiled=True).reshape(
        image_count * requests, model_width
    )
    text_mod = lax.all_to_all(
        jnp.broadcast_to(text_mod_own[None], (owners,) + text_mod_own.shape),
        "tensor",
        0,
        0,
        tiled=True,
    ).reshape(text_tile * requests, model_width)
    tile_index = lax.axis_index("tile")
    token_index = jnp.arange(image_count, dtype=jnp.int32)
    owner = token_index // own_image
    within = token_index % own_image
    row_ids = (anchor[None, :, 0] + tile_index * tile_rows + (within // tile_cols)[:, None]).astype(
        jnp.float32
    )
    col_ids = (anchor[None, :, 1] + (owner * tile_cols + within % tile_cols)[:, None]).astype(
        jnp.float32
    )
    cos_table, sin_table = rope_tables(row_ids.reshape(-1), col_ids.reshape(-1))
    cos_table = cos_table[:, None, :]
    sin_table = sin_table[:, None, :]
    image_qkv = jnp.dot(
        image_mod,
        qkv_image.reshape(model_width, 3 * local_cols),
        preferred_element_type=jnp.float32,
    ).reshape(image_count * requests, 3, local_heads, HEAD_DIM)
    text_qkv = jnp.dot(
        text_mod, qkv_text.reshape(model_width, 3 * local_cols), preferred_element_type=jnp.float32
    ).reshape(text_tile * requests, 3, local_heads, HEAD_DIM)
    token_shape = (block_len, requests, local_heads, HEAD_DIM)
    query = jnp.concatenate(
        [
            head_norm(text_qkv[:, 0], qk_gain[1, 0]).astype(jnp.bfloat16),
            rotate(head_norm(image_qkv[:, 0], qk_gain[0, 0]), cos_table, sin_table).astype(
                jnp.bfloat16
            ),
        ],
        0,
    ).reshape(token_shape)
    keys = jnp.concatenate(
        [
            head_norm(text_qkv[:, 1], qk_gain[1, 1]).astype(jnp.bfloat16),
            rotate(head_norm(image_qkv[:, 1], qk_gain[0, 1]), cos_table, sin_table).astype(
                jnp.bfloat16
            ),
        ],
        0,
    ).reshape(token_shape)
    values = (
        jnp.concatenate([text_qkv[:, 2], image_qkv[:, 2]], 0)
        .astype(jnp.bfloat16)
        .reshape(token_shape)
    )
    score_scale = 1.0 / math.sqrt(HEAD_DIM)
    tiles = lax.axis_size("tile")
    parts = tiles // requests
    part_len = block_len // parts
    keys_r = jnp.repeat(keys.transpose(1, 0, 2, 3), parts, axis=0)
    values_r = jnp.repeat(values.transpose(1, 0, 2, 3), parts, axis=0)
    query_r = query.transpose(1, 0, 2, 3).reshape(tiles, part_len, local_heads, HEAD_DIM)
    outgoing = jnp.concatenate([keys_r, values_r, query_r], 1)
    incoming = lax.all_to_all(outgoing, "tile", 0, 0, tiled=True)
    keys_all = incoming[:, :block_len].reshape(tiles * block_len, local_heads, HEAD_DIM)
    values_all = incoming[:, block_len : 2 * block_len].reshape(
        tiles * block_len, local_heads, HEAD_DIM
    )
    query_mine = incoming[:, 2 * block_len :].reshape(tiles * part_len, local_heads, HEAD_DIM)
    my_request = tile_index // parts
    usable = key_usable(text_len[my_request][None], keys_all.shape[0], text_tile, block_len)[0][
        None, None, :
    ]
    scores = (
        jnp.einsum("qhd,khd->hqk", query_mine, keys_all, preferred_element_type=jnp.float32)
        * score_scale
    )
    row_top = jnp.max(jnp.where(usable, scores, -jnp.inf), -1, keepdims=True)
    weights_raw = jnp.where(usable, jnp.exp(scores - row_top), 0.0)
    weight_sum = jnp.sum(weights_raw, -1, keepdims=True)
    accum = jnp.einsum(
        "hqk,khd->hqd",
        weights_raw.astype(jnp.bfloat16),
        values_all,
        preferred_element_type=jnp.float32,
    )
    attended_mine = (
        (accum / weight_sum)
        .astype(jnp.bfloat16)
        .transpose(1, 0, 2)
        .reshape(tiles, part_len, local_heads * HEAD_DIM)
    )
    returned = lax.all_to_all(attended_mine, "tile", 0, 0, tiled=True)
    attended = returned.reshape(requests, block_len, local_cols).transpose(1, 0, 2)
    text_att = attended[:text_tile].reshape(text_tile * requests, local_cols)
    image_att = attended[text_tile:].reshape(image_count * requests, local_cols)
    image_term = jnp.dot(image_att, proj_image, preferred_element_type=jnp.float32).reshape(
        image_count, requests, model_width
    )
    image_sum = sum_over_tensor(image_term, owners, NARROW_SUMS)
    text_term = jnp.dot(text_att, proj_text, preferred_element_type=jnp.float32).reshape(
        text_tile, requests, model_width
    )
    after_image = (image_sum[0, 0, 0] * 0.0).astype(text_term.dtype)
    text_sum = sum_over_tensor(text_term + after_image, owners, NARROW_SUMS)
    image_mid = (image_own.astype(jnp.float32) + mod_image[None, :, 2, :] * image_sum).astype(
        jnp.bfloat16
    )
    mlp_mod = modulate(image_mid, mod_mlp[None, :, 0, :], mod_mlp[None, :, 1, :])
    piece = lax.all_gather(mlp_mod, "tensor", axis=0, tiled=True)
    grown = jnp.dot(piece.reshape(-1, model_width), mlp_expand, preferred_element_type=jnp.float32)
    activated = jax.nn.gelu(grown, approximate=True).astype(jnp.bfloat16)
    text_out = (text_own.astype(jnp.float32) + mod_text[None, :, 2, :] * text_sum).astype(
        jnp.bfloat16
    )
    mlp_term = jnp.dot(activated, mlp_reduce, preferred_element_type=jnp.float32).reshape(
        image_count, requests, model_width
    )
    mlp_sum = sum_over_tensor(mlp_term, owners, NARROW_SUMS)
    image_out = (image_mid.astype(jnp.float32) + mod_mlp[None, :, 2, :] * mlp_sum).astype(
        jnp.bfloat16
    )
    final_in = modulate(image_out, mod_final[None, :, 0, :], mod_final[None, :, 1, :])
    velocity = jnp.dot(
        final_in.reshape(own_image * requests, model_width),
        final_weight,
        preferred_element_type=jnp.float32,
    ).reshape(own_image, requests, final_weight.shape[1])
    velocity = velocity.transpose(1, 0, 2).reshape(
        requests, tile_rows, tile_cols * final_weight.shape[1]
    )
    step_float = step_index.astype(jnp.float32)
    time_delta = sigma_of(step_float + 1.0) - sigma_of(step_float)
    latents_next = latents + time_delta[:, None, None] * velocity
    latents_ext = padded(latents_next, (("tile", 1),), 1)
    image_out = image_out.transpose(1, 0, 2).reshape(requests, tile_rows, tile_cols, model_width)
    return (image_out, text_out.transpose(1, 0, 2), latents_ext)


def solution(mesh):
    return jax.shard_map(
        per_device,
        mesh=mesh,
        in_specs=(
            P(None, "tile", "tensor", None),
            P(None, ("tile", "tensor"), None),
            P(None, "tile", "tensor"),
            P(),
            P(),
            P(),
            P(),
            P(),
            P(),
            P(),
            P(None, None, "tensor"),
            P(None, None, "tensor"),
            P("tensor", None),
            P("tensor", None),
            P(),
            P(None, "tensor"),
            P("tensor", None),
            P(),
        ),
        out_specs=(
            P(None, "tile", "tensor", None),
            P(None, ("tile", "tensor"), None),
            P(None, "tile", "tensor"),
        ),
        check_vma=False,
    )
```

profile of v0, /device:TPU:97, one launch (start us, length us, event | category | flops | bytes accessed | tf_op | source)
XLA Modules:
  0.0 343.5 jit_solution(16405498130412113823)
XLA Ops:
  7.2 1.1 copy.54
  8.7 1.0 slice_bitcast_fusion.9
  9.7 0.8 add_convert_fusion.1
  10.6 1.0 fusion.66
  12.6 1.3 broadcast_in_dim.42
  13.9 6.8 %all-to-all-start = ((bf16[16,2,8,3072]{3,2,1,0:T(8,128)(2,1)}), bf16[16,2,8,3072]{3,2,1,0:T(8,128)(2,1)}, u32[]{:S(2)}, u32[]{:S(2)}) async-start(bf16[16,2,8,3072]{3,2,1,0:T(8,128)(2,1)} %broadcast_in_dim.42), calls=%async_computation | async-start | bytes 3145728 | tf_op jit(solution)/shard_map/all_to_all | solution.py:126
  20.7 4.3 %copy.57 = bf16[3072,3,128]{0,2,1:T(8,128)(2,1)} copy(bf16[3072,3,128]{2,0,1:T(8,128)(2,1)} %param.28) | data formatting | bytes 4718592 | tf_op args[10]
  25.3 4.3 %copy.56 = bf16[3072,3,128]{0,2,1:T(8,128)(2,1)} copy(bf16[3072,3,128]{2,0,1:T(8,128)(2,1)} %param.29) | data formatting | bytes 4718592 | tf_op args[11]
  31.9 14.3 %all-to-all-done = bf16[16,2,8,3072]{3,2,1,0:T(8,128)(2,1)} async-done(((bf16[16,2,8,3072]{3,2,1,0:T(8,128)(2,1)}), bf16[16,2,8,3072]{3,2,1,0:T(8,128)(2,1)}, u32[]{:S(2)}, u32[]{:S(2)}) %all-to-all-start) | async-done | bytes 1572896 | tf_op jit(solution)/shard_map/all_to_all | solution.py:126
  46.2 3.1 fusion.13
  49.8 0.7 copy.65
  50.5 0.7 copy.62
  51.3 24.4 %all-gather.3.cloned.1.call-done = bf16[64,8,3072]{2,1,0:T(8,128)(2,1)} async-done(((bf16[4,8,3072]{2,1,0:T(8,128)(2,1)}), bf16[64,8,3072]{2,1,0:T(8,128)(2,1)}) %all-gather.3.cloned.1.call-update) | async-done | bytes 3145744 | tf_op jit(solution)/shard_map/all_gather | solution.py:123
  75.7 4.0 %fusion.3 = f32[512,3,128]{0,2,1:T(8,128)S(1)} fusion(bf16[64,8,3072]{2,1,0:T(8,128)(2,1)} %all-gather.3.cloned.1.call-done, bf16[3072,3,128]{0,2,1:T(8,128)(2,1)} %copy.57), kind=kOutput, calls=%fused_computation.10 | convolution fusion | flops 1207959552 | bytes 6291456 | tf_op jit(solution)/shard_map/dot_general | solution.py:146
  80.9 2.1 fusion.60
  83.2 0.9 pad_maximum_fusion.3
  85.0 0.9 pad_maximum_fusion.2
  86.3 2.0 pad_maximum_fusion
  88.3 7.9 %all-to-all-start.1 = ((bf16[16,240,1,128]{3,1,2,0:T(8,128)(2,1)}), bf16[16,240,1,128]{3,1,2,0:T(8,128)(2,1)}, u32[]{:S(2)}, u32[]{:S(2)}) async-start(bf16[16,240,1,128]{3,1,2,0:T(8,128)(2,1)} %pad_maximum_fusion), calls=%async_computation.1 | async-start | bytes 1966080 | tf_op jit(solution)/shard_map/all_to_all | solution.py:186
  97.5 23.7 %all-to-all-done.1 = bf16[16,240,1,128]{3,1,2,0:T(8,128)(2,1)} async-done(((bf16[16,240,1,128]{3,1,2,0:T(8,128)(2,1)}), bf16[16,240,1,128]{3,1,2,0:T(8,128)(2,1)}, u32[]{:S(2)}, u32[]{:S(2)}) %all-to-all-start.1) | async-done | bytes 983072 | tf_op jit(solution)/shard_map/all_to_all | solution.py:186
  121.1 1.2 fusion.105
  122.3 0.9 slice.176
  123.2 0.9 select_reduce_fusion
  124.1 1.1 fusion.1
  125.2 0.9 fusion.19
  126.1 13.0 %all_to_all.30 = bf16[16,48,128]{2,1,0:T(8,128)(2,1)S(1)} all-to-all(bf16[16,48,128]{2,1,0:T(8,128)(2,1)S(1)} %bitcast.211), channel_id=1, replica_groups=mesh['tile'=16,'tensor'=16] {'tile'}, dimensions={0} | all-to-all | bytes 393216 | tf_op jit(solution)/shard_map/all_to_all | solution.py:215
  139.8 2.6 convolution_convert_fusion
  142.5 4.6 %all-to-all-start.3 = ((bf16[16,4,8,3072]{3,2,1,0:T(8,128)(2,1)}), bf16[16,4,8,3072]{3,2,1,0:T(8,128)(2,1)}, u32[]{:S(2)}, u32[]{:S(2)}) async-start(bf16[16,4,8,3072]{3,2,1,0:T(8,128)(2,1)} %bitcast.191), calls=%async_computation.3 | async-start | bytes 6291456 | tf_op jit(solution)/shard_map/all_to_all | solution.py:82
  148.0 46.9 %all-to-all-done.3 = bf16[16,4,8,3072]{3,2,1,0:T(8,128)(2,1)} async-done(((bf16[16,4,8,3072]{3,2,1,0:T(8,128)(2,1)}), bf16[16,4,8,3072]{3,2,1,0:T(8,128)(2,1)}, u32[]{:S(2)}, u32[]{:S(2)}) %all-to-all-start.3) | async-done | bytes 3145760 | tf_op jit(solution)/shard_map/all_to_all | solution.py:82
  194.9 2.5 convert_reduce_fusion.1
  197.9 0.8 fusion.45
  199.9 3.0 fusion
  202.9 4.4 %all-to-all-start.5 = ((bf16[16,2,8,3072]{3,2,1,0:T(8,128)(2,1)}), bf16[16,2,8,3072]{3,2,1,0:T(8,128)(2,1)}, u32[]{:S(2)}, u32[]{:S(2)}) async-start(bf16[16,2,8,3072]{3,2,1,0:T(8,128)(2,1)} %bitcast.192), calls=%async_computation.5 | async-start | bytes 3145728 | tf_op jit(solution)/shard_map/all_to_all | solution.py:82
  207.3 52.4 %all-gather.5.cloned.1.call-done = bf16[64,8,3072]{2,1,0:T(8,128)(2,1)} async-done(((bf16[4,8,3072]{2,1,0:T(8,128)(2,1)}), bf16[64,8,3072]{2,1,0:T(8,128)(2,1)}) %all-gather.5.cloned.1.call-update) | async-done | bytes 3145744 | tf_op jit(solution)/shard_map/all_gather | solution.py:232
  259.7 7.8 %convolution_convert_fusion.1 = bf16[512,3072]{1,0:T(8,128)(2,1)} fusion(bf16[384,3072]{1,0:T(8,128)(2,1)S(1)} %copy-done, bf16[3072,384]{1,0:T(8,128)(2,1)} %param.33, bf16[64,8,3072]{2,1,0:T(8,128)(2,1)} %all-gather.5.cloned.1.call-done), kind=kOutput, calls=%fused_computation.5 | convolution fusion | flops 2419261440 | bytes 11010048 | tf_op jit(solution)/shard_map/dot_general | solution.py:238
  267.5 4.6 %all-to-all-start.4 = ((bf16[16,4,8,3072]{3,2,1,0:T(8,128)(2,1)}), bf16[16,4,8,3072]{3,2,1,0:T(8,128)(2,1)}, u32[]{:S(2)}, u32[]{:S(2)}) async-start(bf16[16,4,8,3072]{3,2,1,0:T(8,128)(2,1)} %bitcast.193), calls=%async_computation.4 | async-start | bytes 6291456 | tf_op jit(solution)/shard_map/all_to_all | solution.py:82
  272.2 1.2 fusion.110
  274.1 1.6 convert_reduce_fusion.2
  275.8 0.7 copy.74
  276.6 41.8 %all-to-all-done.4 = bf16[16,4,8,3072]{3,2,1,0:T(8,128)(2,1)} async-done(((bf16[16,4,8,3072]{3,2,1,0:T(8,128)(2,1)}), bf16[16,4,8,3072]{3,2,1,0:T(8,128)(2,1)}, u32[]{:S(2)}, u32[]{:S(2)}) %all-to-all-start.4) | async-done | bytes 3145760 | tf_op jit(solution)/shard_map/all_to_all | solution.py:82
  318.4 2.5 convert_reduce_fusion
  320.9 1.0 convert_reduce_fusion.4
  322.2 1.3 convolution_bitcast_fusion
  323.7 6.2 %collective-permute-start = (f32[8,1,128]{2,1,0:T(1,128)S(1)}, f32[8,1,128]{2,1,0:T(1,128)S(1)}, u32[]{:S(2)}, u32[]{:S(2)}) collective-permute-start(f32[8,1,128]{2,1,0:T(1,128)S(1)} %get-tuple-element.33), channel_id=1, source_target_pairs={{0,16},{16,32},{32,48},{48,64},{64,80},{80,96},{96,112},{112,128},... | collective-permute-start | bytes 12296 | tf_op jit(solution)/shard_map/ppermute | solution.py:21
  329.9 1.9 collective-permute-start.1
  331.9 1.1 fusion.52
  332.9 0.9 copy.73
  333.8 2.2 collective-permute-done.1
  (116 shorter events, 12.3 us)
Async XLA Ops:
  7.2 252.6 %copy-start = (bf16[384,3072]{1,0:T(8,128)(2,1)S(1)}, bf16[384,3072]{1,0:T(8,128)(2,1)}, u32[]{:S(2)}) copy-start(bf16[384,3072]{1,0:T(8,128)(2,1)} %param.34) | copy-start | bytes 7077892
  7.2 4.4 %copy-start.2 = (bf16[8,2,3072]{2,1,0:T(2,128)(2,1)S(1)}, bf16[8,2,3072]{2,1,0:T(2,128)(2,1)}, u32[]{:S(2)}) copy-start(bf16[8,2,3072]{2,1,0:T(2,128)(2,1)} %param.19) | copy-start | bytes 294916
  7.2 4.6 %copy-start.10 = (f32[8,3,3072]{2,0,1:T(8,128)S(1)}, f32[8,3,3072]{2,0,1:T(8,128)}, u32[]{:S(2)}) copy-start(f32[8,3,3072]{2,0,1:T(8,128)} %param.25) | copy-start | bytes 884740
  7.2 68.5 %all-gather.3.cloned.1.call-start = ((), (), s32[]{:S(2)}) async-start(), calls=%async_computation.6 | async-start | bytes 3342336 | tf_op jit(solution)/shard_map/all_gather | solution.py:123
  13.9 32.3 %all-to-all-start = ((bf16[16,2,8,3072]{3,2,1,0:T(8,128)(2,1)}), bf16[16,2,8,3072]{3,2,1,0:T(8,128)(2,1)}, u32[]{:S(2)}, u32[]{:S(2)}) async-start(bf16[16,2,8,3072]{3,2,1,0:T(8,128)(2,1)} %broadcast_in_dim.42), calls=%async_computation | async-start | bytes 3145728 | tf_op jit(solution)/shard_map/all_to_all | solution.py:126
  20.7 4.3 %copy-start.14 = (s32[8,2]{0,1:T(2,128)S(1)}, s32[8,2]{0,1:T(2,128)}, u32[]{:S(2)}) copy-start(s32[8,2]{0,1:T(2,128)} %param.22) | copy-start | bytes 196
  25.0 6.9 %copy-start.13 = (f32[2,2,128]{2,1,0:T(2,128)S(1)}, f32[2,2,128]{2,1,0:T(2,128)}, u32[]{:S(2)}) copy-start(f32[2,2,128]{2,1,0:T(2,128)} %param.32) | copy-start | bytes 6148
  79.7 1.1 copy-start.15
  79.8 1.1 copy-start.16
  79.8 1.1 copy-start.17
  79.8 1.1 copy-start.18
  79.8 1.0 copy-start.19
  79.8 1.0 copy-start.20
  85.0 11.2 %copy-start.21 = (s32[8]{0:T(128)S(1)}, s32[8]{0:T(128)}, u32[]{:S(2)}) copy-start(s32[8]{0:T(128)} %param.23) | copy-start | bytes 100
  88.3 32.8 %all-to-all-start.1 = ((bf16[16,240,1,128]{3,1,2,0:T(8,128)(2,1)}), bf16[16,240,1,128]{3,1,2,0:T(8,128)(2,1)}, u32[]{:S(2)}, u32[]{:S(2)}) async-start(bf16[16,240,1,128]{3,1,2,0:T(8,128)(2,1)} %pad_maximum_fusion), calls=%async_computation.1 | async-start | bytes 1966080 | tf_op jit(solution)/shard_map/all_to_all | solution.py:186
  125.2 14.6 %copy-start.4 = (bf16[128,3072]{1,0:T(8,128)(2,1)S(1)}, bf16[128,3072]{1,0:T(8,128)(2,1)}, u32[]{:S(2)}) copy-start(bf16[128,3072]{1,0:T(8,128)(2,1)} %param.30) | copy-start | bytes 2359300
  139.1 0.7 copy-start.3
  142.5 4.9 %copy-start.11 = (f32[8,3,3072]{2,0,1:T(8,128)S(1)}, f32[8,3,3072]{2,0,1:T(8,128)}, u32[]{:S(2)}) copy-start(f32[8,3,3072]{2,0,1:T(8,128)} %param.26) | copy-start | bytes 884740
  142.5 52.5 %all-to-all-start.3 = ((bf16[16,4,8,3072]{3,2,1,0:T(8,128)(2,1)}), bf16[16,4,8,3072]{3,2,1,0:T(8,128)(2,1)}, u32[]{:S(2)}, u32[]{:S(2)}) async-start(bf16[16,4,8,3072]{3,2,1,0:T(8,128)(2,1)} %bitcast.191), calls=%async_computation.3 | async-start | bytes 6291456 | tf_op jit(solution)/shard_map/all_to_all | solution.py:82
  147.1 112.6 %all-gather.5.cloned.1.call-start = ((), (), s32[]{:S(2)}) async-start(), calls=%async_computation.7 | async-start | bytes 3342336 | tf_op jit(solution)/shard_map/all_gather | solution.py:232
  194.9 3.0 copy-start.5
  194.9 3.0 copy-start.6
  197.5 5.4 %copy-start.1 = (f32[4,8,3072]{2,1,0:T(8,128)}, f32[4,8,3072]{2,1,0:T(8,128)S(1)}, u32[]{:S(2)}) copy-start(f32[4,8,3072]{2,1,0:T(8,128)S(1)} %convert_reduce_fusion.1) | copy-start | bytes 1179652
  202.9 64.6 %all-to-all-start.5 = ((bf16[16,2,8,3072]{3,2,1,0:T(8,128)(2,1)}), bf16[16,2,8,3072]{3,2,1,0:T(8,128)(2,1)}, u32[]{:S(2)}, u32[]{:S(2)}) async-start(bf16[16,2,8,3072]{3,2,1,0:T(8,128)(2,1)} %bitcast.192), calls=%async_computation.5 | async-start | bytes 3145728 | tf_op jit(solution)/shard_map/all_to_all | solution.py:82
  267.5 4.7 %copy-start.22 = (s32[8]{0:T(128)S(1)}, s32[8]{0:T(128)}, u32[]{:S(2)}) copy-start(s32[8]{0:T(128)} %param.21) | copy-start | bytes 100
  267.5 8.2 %copy-start.9 = (f32[8,3072]{1,0:T(8,128)S(1)}, f32[8,3072]{1,0:T(8,128)}, u32[]{:S(2)}) copy-start(f32[8,3072]{1,0:T(8,128)} %get-tuple-element.14) | copy-start | bytes 294916
  267.5 50.9 %all-to-all-start.4 = ((bf16[16,4,8,3072]{3,2,1,0:T(8,128)(2,1)}), bf16[16,4,8,3072]{3,2,1,0:T(8,128)(2,1)}, u32[]{:S(2)}, u32[]{:S(2)}) async-start(bf16[16,4,8,3072]{3,2,1,0:T(8,128)(2,1)} %bitcast.193), calls=%async_computation.4 | async-start | bytes 6291456 | tf_op jit(solution)/shard_map/all_to_all | solution.py:82
  275.7 47.8 %copy-start.12 = (f32[8,2,128]{2,1,0:T(2,128)S(1)}, f32[8,2,128]{2,1,0:T(2,128)}, u32[]{:S(2)}) copy-start(f32[8,2,128]{2,1,0:T(2,128)} %param.20) | copy-start | bytes 24580
  275.8 46.4 %copy-start.7 = (f32[8,3072]{1,0:T(8,128)S(1)}, f32[8,3072]{1,0:T(8,128)}, u32[]{:S(2)}) copy-start(f32[8,3072]{1,0:T(8,128)} %get-tuple-element.55) | copy-start | bytes 294916
  318.4 3.8 %copy-start.8 = (f32[8,3072]{1,0:T(8,128)S(1)}, f32[8,3072]{1,0:T(8,128)}, u32[]{:S(2)}) copy-start(f32[8,3072]{1,0:T(8,128)} %get-tuple-element.56) | copy-start | bytes 294916
  323.7 10.1 %collective-permute-start = (f32[8,1,128]{2,1,0:T(1,128)S(1)}, f32[8,1,128]{2,1,0:T(1,128)S(1)}, u32[]{:S(2)}, u32[]{:S(2)}) collective-permute-start(f32[8,1,128]{2,1,0:T(1,128)S(1)} %get-tuple-element.33), channel_id=1, source_target_pairs={{0,16},{16,32},{32,48},{48,64},{64,80},{80,96},{96,112},{112,128},... | collective-permute-start | bytes 12296 | tf_op jit(solution)/shard_map/ppermute | solution.py:21
  329.9 6.1 %collective-permute-start.1 = (f32[8,1,128]{2,1,0:T(1,128)S(1)}, f32[8,1,128]{2,1,0:T(1,128)S(1)}, u32[]{:S(2)}, u32[]{:S(2)}) collective-permute-start(f32[8,1,128]{2,1,0:T(1,128)S(1)} %get-tuple-element.34), channel_id=1, source_target_pairs={{16,0},{32,16},{48,32},{64,48},{80,64},{96,80},{112,96},{128,112},... | collective-permute-start | bytes 12296 | tf_op jit(solution)/shard_map/ppermute | solution.py:22
Sparse Core Ops, SparseCore 0:
  11.0 64.6 all-gather.2
  198.8 60.8 all-gather.4
where the time goes:
time: 345 us; the launch traced here: 344 us
  waiting for transfers between devices  206 us (60%)
  starting transfers between devices  36.8 us (11%)
  other arithmetic  27.1 us (8%)
  matrix products  23.7 us (7%)
  local copies, waits for them, and re-layouts  21.9 us (6%)
  between operations  15.2 us (4%)
  blocking collectives  13 us (4%)
    all_to_all x3, waiting for transfers between devices, sum_over_tensor(): parts = lax.all_to_all(parts, 'tensor', 0, 0, tiled=True)  88.7 us
    all_gather x1, waiting for transfers between devices, per_device(): piece = lax.all_gather(mlp_mod, 'tensor', axis=0, tiled=True)  52.4 us
    all_gather x1, waiting for transfers between devices, per_device(): lax.all_gather(image_mod_own, 'tensor', axis=0, tiled=True)  24.4 us
    all_to_all x1, waiting for transfers between devices, per_device(): incoming = lax.all_to_all(outgoing, 'tile', 0, 0, tiled=True)  23.7 us
    all_to_all x1, waiting for transfers between devices, per_device(): lax.all_to_all(jnp.broadcast_to(text_mod_own[None], (owners,) + text_mod_...  14.3 us
    all_to_all x3, starting transfers between devices, sum_over_tensor(): parts = lax.all_to_all(parts, 'tensor', 0, 0, tiled=True)  13.6 us
    all_to_all x1, blocking collectives, per_device(): returned = lax.all_to_all(attended_mine, 'tile', 0, 0, tiled=True)  13 us
    unnamed x50, local copies, waits for them, and re-layouts  11 us
  transfers between devices with their start and end apart: 9, of which 7 were waited for; matrix products, arithmetic and copies ran while one was open for 11% of the time, Pallas kernels for 0%

commit v1 on v0

--- a/solution.py
+++ b/solution.py
@@ -9,6 +9,29 @@
 NSTEPS = 28
 norm_eps = 1e-06
 time_shift = 3.0
+
+
+def split_up(value, dim, count):
+    dims = value.shape
+    pieces = value.reshape(*dims[:dim], count, dims[dim] // count, *dims[dim + 1 :])
+    return jnp.moveaxis(pieces, dim, 0)
+
+
+def joined_along(pieces, dim):
+    lengths = list(pieces.shape[1:])
+    lengths[dim] *= pieces.shape[0]
+    return jnp.moveaxis(pieces, 0, dim).reshape(lengths)
+
+
+def swapped_with_each(x, axis, split_dim, concat_dim):
+    size, index = (lax.axis_size(axis), lax.axis_index(axis))
+    blocks = split_up(x, split_dim, size)
+    finished = [blocks[index]]
+    for lap in range(1, size):
+        sent = blocks[index ^ lap]
+        finished.append(lax.ppermute(sent, axis, [(i, i ^ lap) for i in range(size)]))
+    blocks = jnp.stack(finished)[index ^ jnp.arange(size)]
+    return joined_along(blocks, concat_dim)
 
 
 def padded(value, sides, width):
@@ -183,7 +206,7 @@
     values_r = jnp.repeat(values.transpose(1, 0, 2, 3), parts, axis=0)
     query_r = query.transpose(1, 0, 2, 3).reshape(tiles, part_len, local_heads, HEAD_DIM)
     outgoing = jnp.concatenate([keys_r, values_r, query_r], 1)
-    incoming = lax.all_to_all(outgoing, "tile", 0, 0, tiled=True)
+    incoming = swapped_with_each(outgoing, "tile", 0, 0)
     keys_all = incoming[:, :block_len].reshape(tiles * block_len, local_heads, HEAD_DIM)
     values_all = incoming[:, block_len : 2 * block_len].reshape(
         tiles * block_len, local_heads, HEAD_DIM

time: 345 us -> 354 us (1.026)
  waiting for transfers between devices: 206 us -> 185 us
  starting transfers between devices: 36.8 us -> 55 us
  local copies, waits for them, and re-layouts: 21.9 us -> 36.3 us
    ppermute x0 -> x15, starting transfers between devices: none -> 26.3 us  [swapped_with_each(): lax.ppermute(sent, axis, [(i, i ^ lap) for i in range(size)])]
    all_to_all x1 -> x0, waiting for transfers between devices: 23.7 us -> none  [per_device(): incoming = lax.all_to_all(outgoing, 'tile', 0, 0, tiled=True)]
    unnamed x50 -> x71, local copies, waits for them, and re-layouts: 11 us -> 20.4 us
    all_to_all x1 -> x0, starting transfers between devices: 7.93 us -> none  [per_device(): incoming = lax.all_to_all(outgoing, 'tile', 0, 0, tiled=True)]
    ppermute x0 -> x15, waiting for transfers between devices: none -> 4.29 us  [swapped_with_each(): lax.ppermute(sent, axis, [(i, i ^ lap) for i in range(size)])]
  transfers between devices with their start and end apart: 9 -> 23, of which waited for: 7 -> 8; matrix products, arithmetic and copies ran while one was open for 11% -> 14% of each run, Pallas kernels for 0% -> 0%
where the time goes in v1:
time: 354 us; the launch traced here: 353 us
  waiting for transfers between devices  185 us (52%)
  starting transfers between devices  55 us (16%)
  local copies, waits for them, and re-layouts  36.3 us (10%)
  other arithmetic  24.7 us (7%)
  matrix products  23.7 us (7%)
  between operations  15.4 us (4%)
  blocking collectives  13.2 us (4%)
    all_to_all x3, waiting for transfers between devices, sum_over_tensor(): parts = lax.all_to_all(parts, 'tensor', 0, 0, tiled=True)  88.9 us
    all_gather x1, waiting for transfers between devices, per_device(): piece = lax.all_gather(mlp_mod, 'tensor', axis=0, tiled=True)  52.5 us
    ppermute x15, starting transfers between devices, swapped_with_each(): lax.ppermute(sent, axis, [(i, i ^ lap) for i in range(size)])  26.3 us
    all_gather x1, waiting for transfers between devices, per_device(): lax.all_gather(image_mod_own, 'tensor', axis=0, tiled=True)  24.4 us
    unnamed x71, local copies, waits for them, and re-layouts  20.4 us
    all_to_all x3, starting transfers between devices, sum_over_tensor(): parts = lax.all_to_all(parts, 'tensor', 0, 0, tiled=True)  13.7 us
    all_to_all x1, blocking collectives, per_device(): returned = lax.all_to_all(attended_mine, 'tile', 0, 0, tiled=True)  13.2 us
    all_to_all x1, waiting for transfers between devices, per_device(): lax.all_to_all(jnp.broadcast_to(text_mod_own[None], (owners,) + text_mod_...  12.5 us
  transfers between devices with their start and end apart: 23, of which 8 were waited for; matrix products, arithmetic and copies ran while one was open for 14% of the time, Pallas kernels for 0%

profile of v1, /device:TPU:97, one launch (start us, length us, event | category | flops | bytes accessed | tf_op | source)
XLA Modules:
  0.0 353.0 jit_solution(3263528909424900870)
XLA Ops:
  7.2 1.1 copy.82
  8.7 1.0 slice_bitcast_fusion.9
  10.6 1.0 fusion.66
  12.6 1.3 broadcast_in_dim.42
  13.9 6.8 %all-to-all-start = ((bf16[16,2,8,3072]{3,2,1,0:T(8,128)(2,1)}), bf16[16,2,8,3072]{3,2,1,0:T(8,128)(2,1)}, u32[]{:S(2)}, u32[]{:S(2)}) async-start(bf16[16,2,8,3072]{3,2,1,0:T(8,128)(2,1)} %broadcast_in_dim.42), calls=%async_computation | async-start | bytes 3145728 | tf_op jit(solution)/shard_map/all_to_all | solution.py:149
  20.8 4.3 %copy.85 = bf16[3072,3,128]{0,2,1:T(8,128)(2,1)} copy(bf16[3072,3,128]{2,0,1:T(8,128)(2,1)} %param.28) | data formatting | bytes 4718592 | tf_op args[10]
  25.5 4.3 %copy.84 = bf16[3072,3,128]{0,2,1:T(8,128)(2,1)} copy(bf16[3072,3,128]{2,0,1:T(8,128)(2,1)} %param.29) | data formatting | bytes 4718592 | tf_op args[11]
  33.8 12.5 %all-to-all-done = bf16[16,2,8,3072]{3,2,1,0:T(8,128)(2,1)} async-done(((bf16[16,2,8,3072]{3,2,1,0:T(8,128)(2,1)}), bf16[16,2,8,3072]{3,2,1,0:T(8,128)(2,1)}, u32[]{:S(2)}, u32[]{:S(2)}) %all-to-all-start) | async-done | bytes 1572896 | tf_op jit(solution)/shard_map/all_to_all | solution.py:149
  46.2 3.1 fusion.13
  51.3 24.4 %all-gather.3.cloned.1.call-done = bf16[64,8,3072]{2,1,0:T(8,128)(2,1)} async-done(((bf16[4,8,3072]{2,1,0:T(8,128)(2,1)}), bf16[64,8,3072]{2,1,0:T(8,128)(2,1)}) %all-gather.3.cloned.1.call-update) | async-done | bytes 3145744 | tf_op jit(solution)/shard_map/all_gather | solution.py:146
  75.7 4.0 %fusion.3 = f32[512,3,128]{0,2,1:T(8,128)S(1)} fusion(bf16[64,8,3072]{2,1,0:T(8,128)(2,1)} %all-gather.3.cloned.1.call-done, bf16[3072,3,128]{0,2,1:T(8,128)(2,1)} %copy.85), kind=kOutput, calls=%fused_computation.11 | convolution fusion | flops 1207959552 | bytes 6291456 | tf_op jit(solution)/shard_map/dot_general | solution.py:169
  80.9 1.5 fusion.60
  85.5 1.0 broadcast_in_dim.77
  86.9 1.1 collective-permute-start
  88.2 1.5 collective-permute-start.2
  89.8 2.6 collective-permute-start.4
  93.7 3.5 collective-permute-start.6
  97.8 2.8 collective-permute-start.7
  101.2 2.9 collective-permute-start.8
  106.3 3.8 %collective-permute-start.10 = (bf16[1,240,1,128]{3,1,2,0:T(8,128)(2,1)S(1)}, bf16[1,240,1,128]{3,1,2,0:T(8,128)(2,1)S(1)}, u32[]{:S(2)}, u32[]{:S(2)}) collective-permute-start(bf16[1,240,1,128]{3,1,2,0:T(8,128)(2,1)S(1)} %get-tuple-element.15), channel_id=1, source_target_pairs={{0,176},{16,160},{32,144},{48,128},{64,240},{80,224},{96,208},{112... | collective-permute-start | bytes 184328 | tf_op jit(solution)/shard_map/ppermute | solution.py:32
  110.8 1.7 collective-permute-start.11
  113.2 2.2 collective-permute-start.12
  116.0 2.5 collective-permute-start.13
  122.0 3.6 %collective-permute-done.13 = bf16[1,240,1,128]{3,1,2,0:T(8,128)(2,1)S(1)} collective-permute-done((bf16[1,240,1,128]{3,1,2,0:T(8,128)(2,1)S(1)}, bf16[1,240,1,128]{3,1,2,0:T(8,128)(2,1)S(1)}, u32[]{:S(2)}, u32[]{:S(2)}) %collective-permute-start.13) | collective-permute-done | bytes 61472 | tf_op jit(solution)/shard_map/ppermute | solution.py:32
  127.5 2.8 gather_fusion
  130.3 1.2 fusion.107
  131.5 0.9 slice.178
  133.3 1.1 fusion.1
  135.4 13.2 %all_to_all.25 = bf16[16,48,128]{2,1,0:T(8,128)(2,1)S(1)} all-to-all(bf16[16,48,128]{2,1,0:T(8,128)(2,1)S(1)} %bitcast.262), channel_id=1, replica_groups=mesh['tile'=16,'tensor'=16] {'tile'}, dimensions={0} | all-to-all | bytes 393216 | tf_op jit(solution)/shard_map/all_to_all | solution.py:238
  149.2 2.7 convolution_convert_fusion
  151.9 4.6 %all-to-all-start.2 = ((bf16[16,4,8,3072]{3,2,1,0:T(8,128)(2,1)}), bf16[16,4,8,3072]{3,2,1,0:T(8,128)(2,1)}, u32[]{:S(2)}, u32[]{:S(2)}) async-start(bf16[16,4,8,3072]{3,2,1,0:T(8,128)(2,1)} %bitcast.240), calls=%async_computation.2 | async-start | bytes 6291456 | tf_op jit(solution)/shard_map/all_to_all | solution.py:105
  157.3 47.0 %all-to-all-done.2 = bf16[16,4,8,3072]{3,2,1,0:T(8,128)(2,1)} async-done(((bf16[16,4,8,3072]{3,2,1,0:T(8,128)(2,1)}), bf16[16,4,8,3072]{3,2,1,0:T(8,128)(2,1)}, u32[]{:S(2)}, u32[]{:S(2)}) %all-to-all-start.2) | async-done | bytes 3145760 | tf_op jit(solution)/shard_map/all_to_all | solution.py:105
  204.3 2.5 convert_reduce_fusion.1
  209.3 3.0 fusion
  212.3 4.4 %all-to-all-start.4 = ((bf16[16,2,8,3072]{3,2,1,0:T(8,128)(2,1)}), bf16[16,2,8,3072]{3,2,1,0:T(8,128)(2,1)}, u32[]{:S(2)}, u32[]{:S(2)}) async-start(bf16[16,2,8,3072]{3,2,1,0:T(8,128)(2,1)} %bitcast.241), calls=%async_computation.4 | async-start | bytes 3145728 | tf_op jit(solution)/shard_map/all_to_all | solution.py:105
  216.7 52.5 %all-gather.5.cloned.1.call-done = bf16[64,8,3072]{2,1,0:T(8,128)(2,1)} async-done(((bf16[4,8,3072]{2,1,0:T(8,128)(2,1)}), bf16[64,8,3072]{2,1,0:T(8,128)(2,1)}) %all-gather.5.cloned.1.call-update) | async-done | bytes 3145744 | tf_op jit(solution)/shard_map/all_gather | solution.py:255
  269.1 7.8 %convolution_convert_fusion.1 = bf16[512,3072]{1,0:T(8,128)(2,1)} fusion(bf16[384,3072]{1,0:T(8,128)(2,1)S(1)} %copy-done, bf16[3072,384]{1,0:T(8,128)(2,1)} %param.33, bf16[64,8,3072]{2,1,0:T(8,128)(2,1)} %all-gather.5.cloned.1.call-done), kind=kOutput, calls=%fused_computation.6 | convolution fusion | flops 2419261440 | bytes 11010048 | tf_op jit(solution)/shard_map/dot_general | solution.py:261
  276.9 4.6 %all-to-all-start.3 = ((bf16[16,4,8,3072]{3,2,1,0:T(8,128)(2,1)}), bf16[16,4,8,3072]{3,2,1,0:T(8,128)(2,1)}, u32[]{:S(2)}, u32[]{:S(2)}) async-start(bf16[16,4,8,3072]{3,2,1,0:T(8,128)(2,1)} %bitcast.244), calls=%async_computation.3 | async-start | bytes 6291456 | tf_op jit(solution)/shard_map/all_to_all | solution.py:105
  281.6 1.2 fusion.112
  283.5 1.6 convert_reduce_fusion.2
  286.0 41.8 %all-to-all-done.3 = bf16[16,4,8,3072]{3,2,1,0:T(8,128)(2,1)} async-done(((bf16[16,4,8,3072]{3,2,1,0:T(8,128)(2,1)}), bf16[16,4,8,3072]{3,2,1,0:T(8,128)(2,1)}, u32[]{:S(2)}, u32[]{:S(2)}) %all-to-all-start.3) | async-done | bytes 3145760 | tf_op jit(solution)/shard_map/all_to_all | solution.py:105
  327.8 2.5 convert_reduce_fusion
  330.4 1.0 convert_reduce_fusion.4
  331.6 1.3 convolution_bitcast_fusion
  333.1 6.2 %collective-permute-start.15 = (f32[8,1,128]{2,1,0:T(1,128)S(1)}, f32[8,1,128]{2,1,0:T(1,128)S(1)}, u32[]{:S(2)}, u32[]{:S(2)}) collective-permute-start(f32[8,1,128]{2,1,0:T(1,128)S(1)} %get-tuple-element.49), channel_id=1, source_target_pairs={{0,16},{16,32},{32,48},{48,64},{64,80},{80,96},{96,112},{112,128},... | collective-permute-start | bytes 12296 | tf_op jit(solution)/shard_map/ppermute | solution.py:44
  339.4 1.9 collective-permute-start.16
  341.3 1.1 fusion.52
  343.3 2.2 collective-permute-done.16
  (171 shorter events, 33.7 us)
Async XLA Ops:
  7.2 262.0 %copy-start = (bf16[384,3072]{1,0:T(8,128)(2,1)S(1)}, bf16[384,3072]{1,0:T(8,128)(2,1)}, u32[]{:S(2)}) copy-start(bf16[384,3072]{1,0:T(8,128)(2,1)} %param.34) | copy-start | bytes 7077892
  7.2 4.4 %copy-start.2 = (bf16[8,2,3072]{2,1,0:T(2,128)(2,1)S(1)}, bf16[8,2,3072]{2,1,0:T(2,128)(2,1)}, u32[]{:S(2)}) copy-start(bf16[8,2,3072]{2,1,0:T(2,128)(2,1)} %param.19) | copy-start | bytes 294916
  7.2 4.6 %copy-start.10 = (f32[8,3,3072]{2,0,1:T(8,128)S(1)}, f32[8,3,3072]{2,0,1:T(8,128)}, u32[]{:S(2)}) copy-start(f32[8,3,3072]{2,0,1:T(8,128)} %param.25) | copy-start | bytes 884740
  7.2 68.5 %all-gather.3.cloned.1.call-start = ((), (), s32[]{:S(2)}) async-start(), calls=%async_computation.5 | async-start | bytes 3342336 | tf_op jit(solution)/shard_map/all_gather | solution.py:146
  10.6 10.2 %copy-start.17 = (s32[8,2]{0,1:T(2,128)S(1)}, s32[8,2]{0,1:T(2,128)}, u32[]{:S(2)}) copy-start(s32[8,2]{0,1:T(2,128)} %param.22) | copy-start | bytes 196
  13.9 32.3 %all-to-all-start = ((bf16[16,2,8,3072]{3,2,1,0:T(8,128)(2,1)}), bf16[16,2,8,3072]{3,2,1,0:T(8,128)(2,1)}, u32[]{:S(2)}, u32[]{:S(2)}) async-start(bf16[16,2,8,3072]{3,2,1,0:T(8,128)(2,1)} %broadcast_in_dim.42), calls=%async_computation | async-start | bytes 3145728 | tf_op jit(solution)/shard_map/all_to_all | solution.py:149
  25.1 4.7 %copy-start.24 = (s32[8]{0:T(128)S(1)}, s32[8]{0:T(128)}, u32[]{:S(2)}) copy-start(s32[8]{0:T(128)} %param.23) | copy-start | bytes 100
  25.1 8.1 %copy-start.16 = (f32[2,2,128]{2,1,0:T(2,128)S(1)}, f32[2,2,128]{2,1,0:T(2,128)}, u32[]{:S(2)}) copy-start(f32[2,2,128]{2,1,0:T(2,128)} %param.32) | copy-start | bytes 6148
  51.3 28.6 %copy-start.14 = (f32[128]{0:T(128)S(1)}, f32[128]{0:T(128)}, u32[]{:S(2)}) copy-start(f32[128]{0:T(128)} %get-tuple-element.54) | copy-start | bytes 1540
  51.3 28.6 %copy-start.15 = (f32[128]{0:T(128)S(1)}, f32[128]{0:T(128)}, u32[]{:S(2)}) copy-start(f32[128]{0:T(128)} %get-tuple-element.55) | copy-start | bytes 1540
  79.7 1.1 copy-start.18
  79.8 1.1 copy-start.19
  79.8 1.1 copy-start.20
  79.8 1.1 copy-start.21
  79.8 1.1 copy-start.22
  79.8 1.1 copy-start.23
  79.8 2.6 copy-start.12
  86.9 6.1 %collective-permute-start = (bf16[1,240,1,128]{3,1,2,0:T(8,128)(2,1)S(1)}, bf16[1,240,1,128]{3,1,2,0:T(8,128)(2,1)S(1)}, u32[]{:S(2)}, u32[]{:S(2)}) collective-permute-start(bf16[1,240,1,128]{3,1,2,0:T(8,128)(2,1)S(1)} %get-tuple-element.25), channel_id=1, source_target_pairs={{0,16},{16,0},{32,48},{48,32},{64,80},{80,64},{96,112},{112,96},{1... | collective-permute-start | bytes 184328 | tf_op jit(solution)/shard_map/ppermute | solution.py:32
  88.0 5.8 %collective-permute-start.1 = (bf16[1,240,1,128]{3,1,2,0:T(8,128)(2,1)S(1)}, bf16[1,240,1,128]{3,1,2,0:T(8,128)(2,1)S(1)}, u32[]{:S(2)}, u32[]{:S(2)}) collective-permute-start(bf16[1,240,1,128]{3,1,2,0:T(8,128)(2,1)S(1)} %get-tuple-element.24), channel_id=1, source_target_pairs={{0,32},{16,48},{32,0},{48,16},{64,96},{80,112},{96,64},{112,80},{1... | collective-permute-start | bytes 184328 | tf_op jit(solution)/shard_map/ppermute | solution.py:32
  88.2 9.7 %collective-permute-start.2 = (bf16[1,240,1,128]{3,1,2,0:T(8,128)(2,1)S(1)}, bf16[1,240,1,128]{3,1,2,0:T(8,128)(2,1)S(1)}, u32[]{:S(2)}, u32[]{:S(2)}) collective-permute-start(bf16[1,240,1,128]{3,1,2,0:T(8,128)(2,1)S(1)} %get-tuple-element.23), channel_id=1, source_target_pairs={{0,48},{16,32},{32,16},{48,0},{64,112},{80,96},{96,80},{112,64},{1... | collective-permute-start | bytes 184328 | tf_op jit(solution)/shard_map/ppermute | solution.py:32
  89.7 11.6 %collective-permute-start.3 = (bf16[1,240,1,128]{3,1,2,0:T(8,128)(2,1)S(1)}, bf16[1,240,1,128]{3,1,2,0:T(8,128)(2,1)S(1)}, u32[]{:S(2)}, u32[]{:S(2)}) collective-permute-start(bf16[1,240,1,128]{3,1,2,0:T(8,128)(2,1)S(1)} %get-tuple-element.22), channel_id=1, source_target_pairs={{0,64},{16,80},{32,96},{48,112},{64,0},{80,16},{96,32},{112,48},{1... | collective-permute-start | bytes 184328 | tf_op jit(solution)/shard_map/ppermute | solution.py:32
  89.8 15.0 %collective-permute-start.4 = (bf16[1,240,1,128]{3,1,2,0:T(8,128)(2,1)S(1)}, bf16[1,240,1,128]{3,1,2,0:T(8,128)(2,1)S(1)}, u32[]{:S(2)}, u32[]{:S(2)}) collective-permute-start(bf16[1,240,1,128]{3,1,2,0:T(8,128)(2,1)S(1)} %get-tuple-element.21), channel_id=1, source_target_pairs={{0,80},{16,64},{32,112},{48,96},{64,16},{80,0},{96,48},{112,32},{1... | collective-permute-start | bytes 184328 | tf_op jit(solution)/shard_map/ppermute | solution.py:32
  93.0 13.3 %collective-permute-start.5 = (bf16[1,240,1,128]{3,1,2,0:T(8,128)(2,1)S(1)}, bf16[1,240,1,128]{3,1,2,0:T(8,128)(2,1)S(1)}, u32[]{:S(2)}, u32[]{:S(2)}) collective-permute-start(bf16[1,240,1,128]{3,1,2,0:T(8,128)(2,1)S(1)} %get-tuple-element.20), channel_id=1, source_target_pairs={{0,96},{16,112},{32,64},{48,80},{64,32},{80,48},{96,0},{112,16},{1... | collective-permute-start | bytes 184328 | tf_op jit(solution)/shard_map/ppermute | solution.py:32
  93.7 17.0 %collective-permute-start.6 = (bf16[1,240,1,128]{3,1,2,0:T(8,128)(2,1)S(1)}, bf16[1,240,1,128]{3,1,2,0:T(8,128)(2,1)S(1)}, u32[]{:S(2)}, u32[]{:S(2)}) collective-permute-start(bf16[1,240,1,128]{3,1,2,0:T(8,128)(2,1)S(1)} %get-tuple-element.19), channel_id=1, source_target_pairs={{0,112},{16,96},{32,80},{48,64},{64,48},{80,32},{96,16},{112,0},{1... | collective-permute-start | bytes 184328 | tf_op jit(solution)/shard_map/ppermute | solution.py:32
  97.8 15.3 %collective-permute-start.7 = (bf16[1,240,1,128]{3,1,2,0:T(8,128)(2,1)S(1)}, bf16[1,240,1,128]{3,1,2,0:T(8,128)(2,1)S(1)}, u32[]{:S(2)}, u32[]{:S(2)}) collective-permute-start(bf16[1,240,1,128]{3,1,2,0:T(8,128)(2,1)S(1)} %get-tuple-element.18), channel_id=1, source_target_pairs={{0,128},{16,144},{32,160},{48,176},{64,192},{80,208},{96,224},{112... | collective-permute-start | bytes 184328 | tf_op jit(solution)/shard_map/ppermute | solution.py:32
  101.2 14.7 %collective-permute-start.8 = (bf16[1,240,1,128]{3,1,2,0:T(8,128)(2,1)S(1)}, bf16[1,240,1,128]{3,1,2,0:T(8,128)(2,1)S(1)}, u32[]{:S(2)}, u32[]{:S(2)}) collective-permute-start(bf16[1,240,1,128]{3,1,2,0:T(8,128)(2,1)S(1)} %get-tuple-element.17), channel_id=1, source_target_pairs={{0,144},{16,128},{32,176},{48,160},{64,208},{80,192},{96,240},{112... | collective-permute-start | bytes 184328 | tf_op jit(solution)/shard_map/ppermute | solution.py:32
  104.8 14.3 %collective-permute-start.9 = (bf16[1,240,1,128]{3,1,2,0:T(8,128)(2,1)S(1)}, bf16[1,240,1,128]{3,1,2,0:T(8,128)(2,1)S(1)}, u32[]{:S(2)}, u32[]{:S(2)}) collective-permute-start(bf16[1,240,1,128]{3,1,2,0:T(8,128)(2,1)S(1)} %get-tuple-element.16), channel_id=1, source_target_pairs={{0,160},{16,176},{32,128},{48,144},{64,224},{80,240},{96,192},{112... | collective-permute-start | bytes 184328 | tf_op jit(solution)/shard_map/ppermute | solution.py:32
  106.3 13.8 %collective-permute-start.10 = (bf16[1,240,1,128]{3,1,2,0:T(8,128)(2,1)S(1)}, bf16[1,240,1,128]{3,1,2,0:T(8,128)(2,1)S(1)}, u32[]{:S(2)}, u32[]{:S(2)}) collective-permute-start(bf16[1,240,1,128]{3,1,2,0:T(8,128)(2,1)S(1)} %get-tuple-element.15), channel_id=1, source_target_pairs={{0,176},{16,160},{32,144},{48,128},{64,240},{80,224},{96,208},{112... | collective-permute-start | bytes 184328 | tf_op jit(solution)/shard_map/ppermute | solution.py:32
  110.8 10.0 %collective-permute-start.11 = (bf16[1,240,1,128]{3,1,2,0:T(8,128)(2,1)S(1)}, bf16[1,240,1,128]{3,1,2,0:T(8,128)(2,1)S(1)}, u32[]{:S(2)}, u32[]{:S(2)}) collective-permute-start(bf16[1,240,1,128]{3,1,2,0:T(8,128)(2,1)S(1)} %get-tuple-element.14), channel_id=1, source_target_pairs={{0,192},{16,208},{32,224},{48,240},{64,128},{80,144},{96,160},{112... | collective-permute-start | bytes 184328 | tf_op jit(solution)/shard_map/ppermute | solution.py:32
  113.2 8.2 %collective-permute-start.12 = (bf16[1,240,1,128]{3,1,2,0:T(8,128)(2,1)S(1)}, bf16[1,240,1,128]{3,1,2,0:T(8,128)(2,1)S(1)}, u32[]{:S(2)}, u32[]{:S(2)}) collective-permute-start(bf16[1,240,1,128]{3,1,2,0:T(8,128)(2,1)S(1)} %get-tuple-element.13), channel_id=1, source_target_pairs={{0,208},{16,192},{32,240},{48,224},{64,144},{80,128},{96,176},{112... | collective-permute-start | bytes 184328 | tf_op jit(solution)/shard_map/ppermute | solution.py:32
  116.0 9.6 %collective-permute-start.13 = (bf16[1,240,1,128]{3,1,2,0:T(8,128)(2,1)S(1)}, bf16[1,240,1,128]{3,1,2,0:T(8,128)(2,1)S(1)}, u32[]{:S(2)}, u32[]{:S(2)}) collective-permute-start(bf16[1,240,1,128]{3,1,2,0:T(8,128)(2,1)S(1)} %get-tuple-element.12), channel_id=1, source_target_pairs={{0,224},{16,240},{32,192},{48,208},{64,160},{80,176},{96,128},{112... | collective-permute-start | bytes 184328 | tf_op jit(solution)/shard_map/ppermute | solution.py:32
  119.1 7.8 %collective-permute-start.14 = (bf16[1,240,1,128]{3,1,0,2:T(8,128)(2,1)S(1)}, bf16[1,240,1,128]{3,1,0,2:T(8,128)(2,1)S(1)}, u32[]{:S(2)}, u32[]{:S(2)}) collective-permute-start(bf16[1,240,1,128]{3,1,0,2:T(8,128)(2,1)S(1)} %constant_dynamic-slice_fusion), channel_id=1, source_target_pairs={{0,240},{16,224},{32,208},{48,192},{64,176},{80,160},{96,144},{112... | collective-permute-start | bytes 184328 | tf_op jit(solution)/shard_map/ppermute | solution.py:32
  134.4 14.8 %copy-start.4 = (bf16[128,3072]{1,0:T(8,128)(2,1)S(1)}, bf16[128,3072]{1,0:T(8,128)(2,1)}, u32[]{:S(2)}) copy-start(bf16[128,3072]{1,0:T(8,128)(2,1)} %param.30) | copy-start | bytes 2359300
  151.9 4.7 %copy-start.11 = (f32[8,3,3072]{2,0,1:T(8,128)S(1)}, f32[8,3,3072]{2,0,1:T(8,128)}, u32[]{:S(2)}) copy-start(f32[8,3,3072]{2,0,1:T(8,128)} %param.26) | copy-start | bytes 884740
  151.9 52.4 %all-to-all-start.2 = ((bf16[16,4,8,3072]{3,2,1,0:T(8,128)(2,1)}), bf16[16,4,8,3072]{3,2,1,0:T(8,128)(2,1)}, u32[]{:S(2)}, u32[]{:S(2)}) async-start(bf16[16,4,8,3072]{3,2,1,0:T(8,128)(2,1)} %bitcast.240), calls=%async_computation.2 | async-start | bytes 6291456 | tf_op jit(solution)/shard_map/all_to_all | solution.py:105
  156.5 112.6 %all-gather.5.cloned.1.call-start = ((), (), s32[]{:S(2)}) async-start(), calls=%async_computation.6 | async-start | bytes 3342336 | tf_op jit(solution)/shard_map/all_gather | solution.py:255
  204.3 3.0 copy-start.5
  204.3 3.0 copy-start.6
  206.9 5.4 %copy-start.1 = (f32[4,8,3072]{2,1,0:T(8,128)}, f32[4,8,3072]{2,1,0:T(8,128)S(1)}, u32[]{:S(2)}) copy-start(f32[4,8,3072]{2,1,0:T(8,128)S(1)} %convert_reduce_fusion.1) | copy-start | bytes 1179652
  212.3 64.7 %all-to-all-start.4 = ((bf16[16,2,8,3072]{3,2,1,0:T(8,128)(2,1)}), bf16[16,2,8,3072]{3,2,1,0:T(8,128)(2,1)}, u32[]{:S(2)}, u32[]{:S(2)}) async-start(bf16[16,2,8,3072]{3,2,1,0:T(8,128)(2,1)} %bitcast.241), calls=%async_computation.4 | async-start | bytes 3145728 | tf_op jit(solution)/shard_map/all_to_all | solution.py:105
  276.9 4.7 %copy-start.25 = (s32[8]{0:T(128)S(1)}, s32[8]{0:T(128)}, u32[]{:S(2)}) copy-start(s32[8]{0:T(128)} %param.21) | copy-start | bytes 100
  276.9 8.3 %copy-start.9 = (f32[8,3072]{1,0:T(8,128)S(1)}, f32[8,3072]{1,0:T(8,128)}, u32[]{:S(2)}) copy-start(f32[8,3072]{1,0:T(8,128)} %get-tuple-element.30) | copy-start | bytes 294916
  276.9 50.9 %all-to-all-start.3 = ((bf16[16,4,8,3072]{3,2,1,0:T(8,128)(2,1)}), bf16[16,4,8,3072]{3,2,1,0:T(8,128)(2,1)}, u32[]{:S(2)}, u32[]{:S(2)}) async-start(bf16[16,4,8,3072]{3,2,1,0:T(8,128)(2,1)} %bitcast.244), calls=%async_computation.3 | async-start | bytes 6291456 | tf_op jit(solution)/shard_map/all_to_all | solution.py:105
  285.2 47.9 %copy-start.13 = (f32[8,2,128]{2,1,0:T(2,128)S(1)}, f32[8,2,128]{2,1,0:T(2,128)}, u32[]{:S(2)}) copy-start(f32[8,2,128]{2,1,0:T(2,128)} %param.20) | copy-start | bytes 24580
  285.2 46.4 %copy-start.7 = (f32[8,3072]{1,0:T(8,128)S(1)}, f32[8,3072]{1,0:T(8,128)}, u32[]{:S(2)}) copy-start(f32[8,3072]{1,0:T(8,128)} %get-tuple-element.71) | copy-start | bytes 294916
  327.8 3.8 %copy-start.8 = (f32[8,3072]{1,0:T(8,128)S(1)}, f32[8,3072]{1,0:T(8,128)}, u32[]{:S(2)}) copy-start(f32[8,3072]{1,0:T(8,128)} %get-tuple-element.72) | copy-start | bytes 294916
  333.1 10.1 %collective-permute-start.15 = (f32[8,1,128]{2,1,0:T(1,128)S(1)}, f32[8,1,128]{2,1,0:T(1,128)S(1)}, u32[]{:S(2)}, u32[]{:S(2)}) collective-permute-start(f32[8,1,128]{2,1,0:T(1,128)S(1)} %get-tuple-element.49), channel_id=1, source_target_pairs={{0,16},{16,32},{32,48},{48,64},{64,80},{80,96},{96,112},{112,128},... | collective-permute-start | bytes 12296 | tf_op jit(solution)/shard_map/ppermute | solution.py:44
  339.4 6.1 %collective-permute-start.16 = (f32[8,1,128]{2,1,0:T(1,128)S(1)}, f32[8,1,128]{2,1,0:T(1,128)S(1)}, u32[]{:S(2)}, u32[]{:S(2)}) collective-permute-start(f32[8,1,128]{2,1,0:T(1,128)S(1)} %get-tuple-element.50), channel_id=1, source_target_pairs={{16,0},{32,16},{48,32},{64,48},{80,64},{96,80},{112,96},{128,112},... | collective-permute-start | bytes 12296 | tf_op jit(solution)/shard_map/ppermute | solution.py:45
  (1 other events, 0.7 us)
Sparse Core Ops, SparseCore 0:
  11.0 64.6 all-gather.2
  208.2 60.8 all-gather.4
